TPU v7x, 32 devices: a whole 2x2x4 slice. The times are simulated.
32 devices in a mesh: col: 8 (over y, x, core), row: 4 (over z).
Axes of the slice: x: 2, y: 2, z: 4, core: 2. Of those that a mesh axis runs over, the one named last changes fastest.
Arguments:
- p_blocks: bfloat16 [4, 72, 4096], P('row', 'col'), may hold values from -0.5390625 to 0.5390625
- p_slots: int32 [4, 72], P('row', 'col'), may hold values from 0 to 18, as said below
- out_slots: int32 [4, 104], P('row', 'col'), may hold values from 0 to 18, as said below
Outputs:
- purified: float32 [4, 104, 4096], P('row', 'col')
Inputs may be any that keep to these rules, and one draw needn't show every extreme that they name: `p_slots`: on each device the used slots (entries below 18) come first and name distinct positions; the remaining slots hold 18. Each device uses between half of its 9 slots (rounded up) and all of them, and some device uses all. `out_slots`: on each device the used slots (entries below 18) come first and name distinct positions; the remaining slots hold 18. Each device uses between half of its 13 slots (rounded up) and all of them, and some device uses all.
All inputs are finite; a program needn't handle non-finite values.
Results may differ from a plain program's by a relative error of at most 0.0003.
Values may be sent and summed in bfloat16 or wider, within the bound.
No kernel may reach another device: no remote copies, remote signals or barrier semaphores. Data moves between devices by JAX's collectives and lax.ppermute only.
A program may use at most 192 MiB of HBM per device.

v0:
```python
import jax
import jax.numpy as jnp
from jax import lax
from jax.sharding import PartitionSpec as P

BLK = 64
COLS_DEV = 3


def on_device(p_blocks, p_slots, out_slots):
    n_row = lax.axis_size("row")
    n_col = lax.axis_size("col")
    capacity = p_slots.shape[1]
    block_edge = BLK
    area = block_edge * block_edge
    rows_dev = COLS_DEV * n_col // n_row
    cells = rows_dev * COLS_DEV
    blocks_total = rows_dev * n_row
    width = COLS_DEV * block_edge
    height = rows_dev * block_edge
    own_ids = p_slots[0]
    id_row = jnp.zeros((1, area), jnp.bfloat16)
    id_row = id_row.at[0, :capacity].set(own_ids.astype(jnp.bfloat16))
    payload = jnp.concatenate([p_blocks[0], id_row], axis=0)
    down = lax.all_gather(payload, "row", axis=0, tiled=False)
    down_ids = down[:, capacity, :capacity].astype(jnp.int32)
    down_row = jnp.arange(n_row, dtype=jnp.int32)[:, None] * rows_dev + down_ids // COLS_DEV
    down_index = jnp.where(
        down_ids < cells, down_row * COLS_DEV + down_ids % COLS_DEV, blocks_total * COLS_DEV
    )
    column_grid = jnp.zeros((blocks_total * COLS_DEV, area), jnp.bfloat16)
    column_grid = column_grid.at[down_index.reshape(-1)].set(
        down[:, :capacity].reshape(n_row * capacity, area), mode="drop"
    )
    column_panel = (
        column_grid.reshape(blocks_total, COLS_DEV, block_edge, block_edge)
        .transpose(0, 2, 1, 3)
        .reshape(blocks_total * block_edge, width)
    )
    across = lax.all_gather(payload, "col", axis=0, tiled=False)
    across_ids = across[:, capacity, :capacity].astype(jnp.int32)
    across_col = jnp.arange(n_col, dtype=jnp.int32)[:, None] * COLS_DEV + across_ids % COLS_DEV
    across_index = jnp.where(
        across_ids < cells,
        across_ids // COLS_DEV * blocks_total + across_col,
        rows_dev * blocks_total,
    )
    row_grid = jnp.zeros((rows_dev * blocks_total, area), jnp.bfloat16)
    row_grid = row_grid.at[across_index.reshape(-1)].set(
        across[:, :capacity].reshape(n_col * capacity, area), mode="drop"
    )
    row_panel = (
        row_grid.reshape(rows_dev, blocks_total, block_edge, block_edge)
        .transpose(0, 2, 1, 3)
        .reshape(height, blocks_total * block_edge)
    )
    square = jnp.dot(row_panel, column_panel, preferred_element_type=jnp.float32)
    square_panel = lax.all_gather(square, "row", axis=0, tiled=True)
    cube = jnp.dot(
        row_panel.astype(jnp.float32),
        square_panel,
        precision=lax.Precision.HIGHEST,
        preferred_element_type=jnp.float32,
    )
    combined = 3.0 * square - 2.0 * cube
    new_grid = combined.reshape(rows_dev, block_edge, COLS_DEV, block_edge).transpose(0, 2, 1, 3)
    new_grid = new_grid.reshape(cells, area)
    out_ids = out_slots[0]
    picked = new_grid[jnp.minimum(out_ids, cells - 1)]
    picked = jnp.where((out_ids < cells)[:, None], picked, jnp.zeros_like(picked))
    return picked[None]


def solution(mesh):
    in_specs = (P("row", "col", None), P("row", "col"), P("row", "col"))
    out_specs = P("row", "col", None)
    return jax.shard_map(
        on_device, mesh=mesh, in_specs=in_specs, out_specs=out_specs, check_vma=False
    )
```

profile of v0, /device:TPU:0, one launch (start us, length us, event | category | flops | bytes accessed | tf_op | source)
XLA Modules:
  0.0 100.4 jit_solution(6214441134641464494)
XLA Ops:
  6.5 0.0 all-gather.6.cloned.1.call-start
  6.5 0.6 compare_reduce_fusion.4
  7.2 1.3 %broadcast_select_fusion = bf16[1,9]{1,0:T(2,128)(2,1)S(1)} fusion(pred[]{:T(512)} %compare_reduce_fusion.4, s32[1,9]{1,0:T(1,128)} %param.6), kind=kLoop, calls=%fused_computation.34 | loop fusion | flops 18 | bytes 55 | tf_op jit(solution)/shard_map/select.3
  8.5 0.9 fusion.7
  9.4 12.4 %all-gather.2 = bf16[8,10,4096]{2,1,0:T(8,128)(2,1)S(1)} all-gather(bf16[1,10,4096]{2,1,0:T(8,128)(2,1)S(1)} %fusion.7), channel_id=2, replica_groups=mesh['col'=8,'row'=4] {'col'}, dimensions={0}, use_global_device_ids=true | all-gather | bytes 737280 | tf_op jit(solution)/shard_map/all_gather | solution.py:40
  21.9 16.3 %all-gather.3 = bf16[4,10,4096]{2,1,0:T(8,128)(2,1)S(1)} all-gather(bf16[1,10,4096]{2,1,0:T(8,128)(2,1)S(1)} %fusion.7), channel_id=3, replica_groups=mesh['col'=8,'row'=4] {'row'}, dimensions={0}, use_global_device_ids=true | all-gather | bytes 409600 | tf_op jit(solution)/shard_map/all_gather | solution.py:25
  38.3 0.0 copy-start
  38.3 0.8 copy-done
  39.1 0.5 compare_reduce_fusion.2
  39.6 0.1 div.35
  39.7 0.1 rem.56
  39.8 0.1 lt.92
  39.9 0.1 ne.104
  40.0 0.1 add.140
  40.0 0.1 add.141
  40.1 0.3 reshape.316
  40.4 1.8 %scatter_custom_fusion = bf16[144,4096]{1,0:T(8,128)(2,1)S(1)} fusion(s32[72]{0:T(128)S(1)} %fusion.12, bf16[72,4096]{1,0:T(8,128)(2,1)S(1)} %reshape.316, bf16[]{:T(256)} %constant.75.clone.1), kind=kCustom, calls=%fused_computation.5 | custom fusion | bytes 1179650 | tf_op jit(solution)/shard_map/scatter | solution.py:49
  42.2 2.6 %reshape.297 = bf16[6,24,64,64]{3,2,1,0:T(8,128)(2,1)S(1)} reshape(bf16[144,4096]{1,0:T(8,128)(2,1)S(1)} %scatter_custom_fusion) | data formatting | bytes 2359296 | tf_op jit(solution)/shard_map/reshape | solution.py:53
  44.8 2.9 %copy.12 = bf16[6,64,24,64]{3,2,1,0:T(8,128)(2,1)} copy(bf16[6,64,24,64]{3,1,2,0:T(8,128)(2,1)S(1)} %bitcast.34) | data formatting | bytes 2359296 | tf_op jit(solution)/shard_map/transpose | solution.py:54
  47.7 0.0 copy-start.2
  47.7 0.0 copy-start.1
  47.7 3.5 %reshape.298 = bf16[384,1536]{1,0:T(8,128)(2,1)S(1)} reshape(bf16[6,64,24,64]{3,2,1,0:T(8,128)(2,1)} %copy.12) | data formatting | bytes 2359296 | tf_op jit(solution)/shard_map/reshape | solution.py:55
  51.3 0.1 div.37
  51.3 0.1 rem.60
  51.4 0.0 copy-done.2
  51.4 0.1 lt.97
  51.5 0.1 ne.109
  51.6 0.1 add.146
  51.7 0.1 add.147
  51.8 0.0 copy-done.1
  51.8 0.1 reshape.324
  51.9 1.2 %scatter_custom_fusion.1 = bf16[72,4096]{1,0:T(8,128)(2,1)S(1)} fusion(s32[36]{0:T(128)S(1)} %fusion.13, bf16[36,4096]{1,0:T(8,128)(2,1)S(1)} %reshape.324, bf16[]{:T(256)} %constant.75.clone.1), kind=kCustom, calls=%fused_computation.7 | custom fusion | bytes 589826 | tf_op jit(solution)/shard_map/scatter | solution.py:32
  53.1 1.3 %reshape.300 = bf16[24,3,64,64]{3,2,1,0:T(8,128)(2,1)S(1)} reshape(bf16[72,4096]{1,0:T(8,128)(2,1)S(1)} %scatter_custom_fusion.1) | data formatting | bytes 1179648 | tf_op jit(solution)/shard_map/reshape | solution.py:36
  54.4 1.3 %copy.13 = bf16[24,64,3,64]{1,0,3,2:T(8,128)(2,1)S(1)} copy(bf16[24,64,3,64]{3,1,2,0:T(8,128)(2,1)S(1)} %bitcast.35) | data formatting | bytes 1179648 | tf_op jit(solution)/shard_map/transpose | solution.py:37
  55.7 0.7 reshape.301
  56.4 0.0 copy-start.3
  56.4 1.3 %fusion.15 = f32[384,192]{0,1:T(8,128)} fusion(bf16[384,1536]{1,0:T(8,128)(2,1)S(1)} %reshape.298, bf16[1536,192]{0,1:T(8,128)(2,1)S(1)} %reshape.301), kind=kOutput, calls=%fused_computation.44 | convolution fusion | flops 226492416 | bytes 2064384 | tf_op jit(solution)/shard_map/dot_general | solution.py:57
  57.7 0.0 all-gather.6.cloned.1.call-update
  57.7 0.0 copy-done.3
  57.8 30.9 %all-gather.6.cloned.1.call-done = f32[1536,192]{0,1:T(8,128)} async-done(((f32[384,192]{0,1:T(8,128)}), f32[1536,192]{0,1:T(8,128)}) %all-gather.6.cloned.1.call-update) | async-done | bytes 1179664 | tf_op jit(solution)/shard_map/all_gather | solution.py:58
  88.7 2.6 %fusion = f32[384,192]{0,1:T(8,128)S(1)} fusion(bf16[384,1536]{1,0:T(8,128)(2,1)S(1)} %reshape.298, f32[1536,192]{0,1:T(8,128)} %all-gather.6.cloned.1.call-done, f32[384,192]{0,1:T(8,128)} %fusion.15), kind=kOutput, calls=%fused_computation.4 | convolution fusion | flops 1359175680 | bytes 2949120 | tf_op jit(solution)/shard_map/dot_general | solution.py:59
  91.3 0.2 reshape.302
  91.4 0.3 copy.14
  91.7 0.2 reshape.303
  91.9 0.6 gather_fusion
  92.5 0.1 bitcast_select_fusion
  92.6 0.9 copy.15
  (10 shorter events, 0.2 us)
Async XLA Ops:
  6.5 82.2 %all-gather.6.cloned.1.call-start = ((), (), s32[]{:S(2)}) async-start(), calls=%async_computation | async-start | bytes 1474560 | tf_op jit(solution)/shard_map/all_gather | solution.py:58
  38.3 0.8 copy-start
  47.7 3.7 %copy-start.2 = (pred[4,9]{1,0:T(4,128)(4,1)S(1)}, pred[4,9]{1,0:T(4,128)(4,1)}, u32[]{:S(2)}) copy-start(pred[4,9]{1,0:T(4,128)(4,1)} %get-tuple-element.22) | copy-start | bytes 112
  47.7 4.0 %copy-start.1 = (bf16[4,10,4096]{2,1,0:T(8,128)(2,1)S(1)}, bf16[4,10,4096]{2,1,0:T(8,128)(2,1)}, u32[]{:S(2)}) copy-start(bf16[4,10,4096]{2,1,0:T(8,128)(2,1)} %copy-done) | copy-start | bytes 983044
  56.4 1.3 %copy-start.3 = (s32[1,13]{1,0:T(1,128)S(1)}, s32[1,13]{1,0:T(1,128)}, u32[]{:S(2)}) copy-start(s32[1,13]{1,0:T(1,128)} %param.7) | copy-start | bytes 160
Sparse Core Ops, SparseCore 0:
  57.9 30.7 all-gather.5
where the time goes:
time: 101 us; the launch traced here: 100 us
  waiting for transfers between devices  30.9 us (31%)
  blocking collectives  28.8 us (29%)
  local copies, waits for them, and re-layouts  19.6 us (19%)
  between operations  13.6 us (13%)
  matrix products  3.83 us (4%)
  other arithmetic  3.67 us (4%)
    all_gather x1, waiting for transfers between devices, on_device(): square_panel = lax.all_gather(square, 'row', axis=0, tiled=True)  30.9 us
    all_gather x1, blocking collectives, on_device(): down = lax.all_gather(payload, 'row', axis=0, tiled=False)  16.3 us
    all_gather x1, blocking collectives, on_device(): across = lax.all_gather(payload, 'col', axis=0, tiled=False)  12.4 us
    reshape x1, local copies, waits for them, and re-layouts, on_device(): row_panel = row_grid.reshape(rows_dev, blocks_total, block_edge, block_ed...  3.5 us
    transpose x1, local copies, waits for them, and re-layouts, on_device(): row_panel = row_grid.reshape(rows_dev, blocks_total, block_edge, block_ed...  2.94 us
    reshape x1, local copies, waits for them, and re-layouts, on_device(): row_grid.reshape(rows_dev, blocks_total, block_edge, block_edge)  2.57 us
    dot_general x1, matrix products, on_device(): jnp.dot(row_panel.astype(jnp.float32), square_panel, precision=lax.Precis...  2.56 us
  transfers between devices with their start and end apart: 1, of which 1 were waited for; matrix products, arithmetic and copies ran while one was open for 0% of the time, Pallas kernels for 0%

commit v1 on v0

--- a/solution.py
+++ b/solution.py
@@ -2,6 +2,7 @@
 import jax.numpy as jnp
 from jax import lax
 from jax.sharding import PartitionSpec as P
+from jax.lax import axis_index, axis_size, ppermute
 
 BLK = 64
 COLS_DEV = 3
@@ -55,7 +56,30 @@
         .reshape(height, blocks_total * block_edge)
     )
     square = jnp.dot(row_panel, column_panel, preferred_element_type=jnp.float32)
-    square_panel = lax.all_gather(square, "row", axis=0, tiled=True)
+    a_next, view_out, frame_out = (axis_size("row"), axis_index("row"), square.shape[0])
+    tray = []
+    for rr, pp in enumerate(square.shape):
+        tray.append(pp * a_next if rr == 0 else pp)
+    w2 = step_out = square
+    square_panel = lax.dynamic_update_slice_in_dim(
+        jnp.zeros(tray, square.dtype), square, view_out * frame_out, axis=0
+    )
+    for it in [*range(1, a_next // 2 + 1)]:
+        column = []
+        for rr in [*range(a_next)]:
+            column.append((rr, (rr + 1) % a_next))
+        w2 = ppermute(w2, "row", column)
+        square_panel = lax.dynamic_update_slice_in_dim(
+            square_panel, w2, (view_out - it) % a_next * frame_out, axis=0
+        )
+        if 2 * it < a_next:
+            row_list = []
+            for rr in tuple(range(a_next)):
+                row_list.append((rr, (rr - 1) % a_next))
+            step_out = ppermute(step_out, "row", row_list)
+            square_panel = lax.dynamic_update_slice_in_dim(
+                square_panel, step_out, (view_out + it) % a_next * frame_out, axis=0
+            )
     cube = jnp.dot(
         row_panel.astype(jnp.float32),
         square_panel,

time: 101 us -> 78 us (0.77)
  between operations: 13.6 us -> 0.22 us
  waiting for transfers between devices: 30.9 us -> 18.2 us
  starting transfers between devices: 0.01 us -> 4.01 us
  matrix products: 3.83 us -> 1.79 us
  local copies, waits for them, and re-layouts: 19.6 us -> 21 us
    all_gather x1 -> x0, waiting for transfers between devices: 30.9 us -> none  [on_device(): square_panel = lax.all_gather(square, 'row', axis=0, tiled=True)]
    ppermute x0 -> x3, waiting for transfers between devices: none -> 18.2 us  [the longest x2 14.8 us: on_device(): w2 = ppermute(w2, 'row', column)]
    ppermute x0 -> x3, starting transfers between devices: none -> 4.01 us  [the longest x1 2.04 us: on_device(): step_out = ppermute(step_out, 'row', row_list)]
    dot_general x1, matrix products: 2.56 us -> 1.25 us  [on_device(): jnp.dot(row_panel.astype(jnp.float32), square_panel, precision=lax.Precis...]
  transfers between devices with their start and end apart: 1 -> 3, of which waited for: 1 -> 3; matrix products, arithmetic and copies ran while one was open for 0% -> 0% of each run, Pallas kernels for 0% -> 0%
where the time goes in v1:
time: 78 us; the launch traced here: 77.7 us
  blocking collectives  28.8 us (37%)
  local copies, waits for them, and re-layouts  21 us (27%)
  waiting for transfers between devices  18.2 us (23%)
  starting transfers between devices  4.01 us (5%)
  other arithmetic  3.72 us (5%)
  matrix products  1.79 us (2%)
    all_gather x1, blocking collectives, on_device(): down = lax.all_gather(payload, 'row', axis=0, tiled=False)  16.3 us
    ppermute x2, waiting for transfers between devices, on_device(): w2 = ppermute(w2, 'row', column)  14.8 us
    all_gather x1, blocking collectives, on_device(): across = lax.all_gather(payload, 'col', axis=0, tiled=False)  12.4 us
    reshape x1, local copies, waits for them, and re-layouts, on_device(): row_panel = row_grid.reshape(rows_dev, blocks_total, block_edge, block_ed...  3.5 us
    ppermute x1, waiting for transfers between devices, on_device(): step_out = ppermute(step_out, 'row', row_list)  3.33 us
    transpose x1, local copies, waits for them, and re-layouts, on_device(): row_panel = row_grid.reshape(rows_dev, blocks_total, block_edge, block_ed...  2.94 us
    reshape x1, local copies, waits for them, and re-layouts, on_device(): row_grid.reshape(rows_dev, blocks_total, block_edge, block_edge)  2.57 us
    ppermute x1, starting transfers between devices, on_device(): step_out = ppermute(step_out, 'row', row_list)  2.04 us
  transfers between devices with their start and end apart: 3, of which 3 were waited for; matrix products, arithmetic and copies ran while one was open for 0% of the time, Pallas kernels for 0%

profile of v1, /device:TPU:0, one launch (start us, length us, event | category | flops | bytes accessed | tf_op | source)
XLA Modules:
  0.0 77.7 jit_solution(1348604308676127025)
XLA Ops:
  0.0 0.6 compare_reduce_fusion.4
  0.6 1.3 %broadcast_select_fusion = bf16[1,9]{1,0:T(2,128)(2,1)S(1)} fusion(pred[]{:T(512)} %compare_reduce_fusion.4, s32[1,9]{1,0:T(1,128)} %param.6), kind=kLoop, calls=%fused_computation.38 | loop fusion | flops 18 | bytes 55 | tf_op jit(solution)/shard_map/select.9
  1.9 0.9 %fusion.7 = bf16[1,10,4096]{2,1,0:T(8,128)(2,1)S(1)} fusion(bf16[1,9]{1,0:T(2,128)(2,1)S(1)} %broadcast_select_fusion, bf16[9,4096]{1,0:T(8,128)(2,1)} %bitcast.39), kind=kLoop, calls=%fused_computation.13 | loop fusion | flops 245760 | bytes 155666
  2.9 12.4 %all-gather.2 = bf16[8,10,4096]{2,1,0:T(8,128)(2,1)S(1)} all-gather(bf16[1,10,4096]{2,1,0:T(8,128)(2,1)S(1)} %fusion.7), channel_id=2, replica_groups=mesh['col'=8,'row'=4] {'col'}, dimensions={0}, use_global_device_ids=true | all-gather | bytes 737280 | tf_op jit(solution)/shard_map/all_gather | solution.py:41
  15.4 16.3 %all-gather.3 = bf16[4,10,4096]{2,1,0:T(8,128)(2,1)S(1)} all-gather(bf16[1,10,4096]{2,1,0:T(8,128)(2,1)S(1)} %fusion.7), channel_id=3, replica_groups=mesh['col'=8,'row'=4] {'row'}, dimensions={0}, use_global_device_ids=true | all-gather | bytes 409600 | tf_op jit(solution)/shard_map/all_gather | solution.py:26
  31.7 0.0 copy-start.1
  31.7 0.6 compare_reduce_fusion.2
  32.3 0.2 copy-done.1
  32.6 0.1 lt.118
  32.7 0.1 add.167
  32.8 0.1 add.168
  32.8 0.1 rem.96
  32.9 0.1 div.35
  33.0 0.1 ne.118
  33.1 0.3 reshape.316
  33.4 1.8 %scatter_custom_fusion = bf16[144,4096]{1,0:T(8,128)(2,1)S(1)} fusion(s32[72]{0:T(128)S(1)} %fusion.12, bf16[72,4096]{1,0:T(8,128)(2,1)S(1)} %reshape.316, bf16[]{:T(256)} %constant.104.clone.1), kind=kCustom, calls=%fused_computation.5 | custom fusion | bytes 1179650 | tf_op jit(solution)/shard_map/scatter | solution.py:50
  35.2 2.6 %reshape.297 = bf16[6,24,64,64]{3,2,1,0:T(8,128)(2,1)S(1)} reshape(bf16[144,4096]{1,0:T(8,128)(2,1)S(1)} %scatter_custom_fusion) | data formatting | bytes 2359296 | tf_op jit(solution)/shard_map/reshape | solution.py:54
  37.8 2.9 %copy.12 = bf16[6,64,24,64]{3,2,1,0:T(8,128)(2,1)} copy(bf16[6,64,24,64]{3,1,2,0:T(8,128)(2,1)S(1)} %bitcast.34) | data formatting | bytes 2359296 | tf_op jit(solution)/shard_map/transpose | solution.py:55
  40.7 0.0 copy-start.3
  40.7 0.0 copy-start.2
  40.7 3.5 %reshape.298 = bf16[384,1536]{1,0:T(8,128)(2,1)S(1)} reshape(bf16[6,64,24,64]{3,2,1,0:T(8,128)(2,1)} %copy.12) | data formatting | bytes 2359296 | tf_op jit(solution)/shard_map/reshape | solution.py:56
  44.2 0.0 copy-done.3
  44.2 0.1 lt.123
  44.3 0.1 rem.100
  44.4 0.1 add.173
  44.5 0.1 add.174
  44.6 0.1 div.37
  44.6 0.1 ne.123
  44.7 0.0 copy-done.2
  44.7 0.1 reshape.324
  44.9 1.2 %scatter_custom_fusion.1 = bf16[72,4096]{1,0:T(8,128)(2,1)S(1)} fusion(s32[36]{0:T(128)S(1)} %fusion.13, bf16[36,4096]{1,0:T(8,128)(2,1)S(1)} %reshape.324, bf16[]{:T(256)} %constant.104.clone.1), kind=kCustom, calls=%fused_computation.7 | custom fusion | bytes 589826 | tf_op jit(solution)/shard_map/scatter | solution.py:33
  46.1 1.3 %reshape.300 = bf16[24,3,64,64]{3,2,1,0:T(8,128)(2,1)S(1)} reshape(bf16[72,4096]{1,0:T(8,128)(2,1)S(1)} %scatter_custom_fusion.1) | data formatting | bytes 1179648 | tf_op jit(solution)/shard_map/reshape | solution.py:37
  47.4 1.3 %copy.13 = bf16[24,64,3,64]{1,0,3,2:T(8,128)(2,1)S(1)} copy(bf16[24,64,3,64]{3,1,2,0:T(8,128)(2,1)S(1)} %bitcast.35) | data formatting | bytes 1179648 | tf_op jit(solution)/shard_map/transpose | solution.py:38
  48.7 1.5 %reshape.301 = bf16[1536,192]{0,1:T(8,128)(2,1)} reshape(bf16[24,64,3,64]{1,0,3,2:T(8,128)(2,1)S(1)} %copy.13) | data formatting | bytes 1179648 | tf_op jit(solution)/shard_map/reshape | solution.py:39
  50.2 0.0 copy-start
  50.2 0.1 broadcast_in_dim.41
  50.3 0.9 %copy-done = bf16[1536,192]{0,1:T(8,128)(2,1)S(1)} copy-done((bf16[1536,192]{0,1:T(8,128)(2,1)S(1)}, bf16[1536,192]{0,1:T(8,128)(2,1)}, u32[]{:S(2)}) %copy-start) | copy-done | bytes 589848
  51.3 0.0 copy-start.4
  51.3 0.5 constant_dynamic-update-slice_fusion.3
  51.8 1.9 %collective-permute-start = (f32[384,192]{0,1:T(8,128)S(1)}, f32[384,192]{0,1:T(8,128)S(1)}, u32[]{:S(2)}, u32[]{:S(2)}) collective-permute-start(f32[384,192]{0,1:T(8,128)S(1)} %get-tuple-element.26), channel_id=1, source_target_pairs={{0,1},{1,2},{2,3},{3,0},{4,5},{5,6},{6,7},{7,4},{8,9},{9,10},{10,1... | collective-permute-start | bytes 884744 | tf_op jit(solution)/shard_map/ppermute | solution.py:71
  53.8 2.0 %collective-permute-start.1 = (f32[384,192]{0,1:T(8,128)S(1)}, f32[384,192]{0,1:T(8,128)S(1)}, u32[]{:S(2)}, u32[]{:S(2)}) collective-permute-start(f32[384,192]{0,1:T(8,128)S(1)} %get-tuple-element.26), channel_id=1, source_target_pairs={{0,3},{1,0},{2,1},{3,2},{4,7},{5,4},{6,5},{7,6},{8,11},{9,8},{10,9... | collective-permute-start | bytes 884744 | tf_op jit(solution)/shard_map/ppermute | solution.py:79
  55.8 0.0 copy-done.4
  55.8 7.8 %collective-permute-done = f32[384,192]{0,1:T(8,128)S(1)} collective-permute-done((f32[384,192]{0,1:T(8,128)S(1)}, f32[384,192]{0,1:T(8,128)S(1)}, u32[]{:S(2)}, u32[]{:S(2)}) %collective-permute-start) | collective-permute-done | bytes 294944 | tf_op jit(solution)/shard_map/ppermute | solution.py:71
  63.6 0.0 collective-permute-start.2
  63.7 3.3 %collective-permute-done.1 = f32[384,192]{0,1:T(8,128)S(1)} collective-permute-done((f32[384,192]{0,1:T(8,128)S(1)}, f32[384,192]{0,1:T(8,128)S(1)}, u32[]{:S(2)}, u32[]{:S(2)}) %collective-permute-start.1) | collective-permute-done | bytes 294944 | tf_op jit(solution)/shard_map/ppermute | solution.py:79
  67.1 7.1 %collective-permute-done.2 = f32[384,192]{0,1:T(8,128)S(1)} collective-permute-done((f32[384,192]{0,1:T(8,128)S(1)}, f32[384,192]{0,1:T(8,128)S(1)}, u32[]{:S(2)}, u32[]{:S(2)}) %collective-permute-start.2) | collective-permute-done | bytes 294944 | tf_op jit(solution)/shard_map/ppermute | solution.py:71
  74.2 1.2 %fusion = f32[384,192]{0,1:T(8,128)S(1)} fusion(bf16[384,1536]{1,0:T(8,128)(2,1)S(1)} %reshape.298, f32[1536,192]{0,1:T(8,128)S(1)} %constant_dynamic-update-slice_fusion, f32[384,192]{0,1:T(8,128)S(1)} %get-tuple-element.26), kind=kOutput, calls=%fused_computation.4 | convolution fusion | flops 1359175680 | bytes 2949120 | tf_op jit(solution)/shard_map/dot_general | solution.py:83
  75.4 0.2 reshape.302
  75.6 0.3 copy.14
  75.9 0.2 reshape.303
  76.1 0.6 gather_fusion
  76.7 0.1 bitcast_select_fusion
  76.8 0.9 %copy.15 = f32[1,13,4096]{2,0,1:T(1,128)} copy(f32[1,13,4096]{2,1,0:T(8,128)S(1)} %bitcast_select_fusion) | data formatting | bytes 425984 | tf_op jit(solution)/shard_map/jit(_where)/select_n | solution.py:94
  (13 shorter events, 0.2 us)
Async XLA Ops:
  31.7 0.8 %copy-start.1 = (bf16[4,10,4096]{2,1,0:T(8,128)(2,1)}, bf16[4,10,4096]{2,1,0:T(8,128)(2,1)S(1)}, u32[]{:S(2)}) copy-start(bf16[4,10,4096]{2,1,0:T(8,128)(2,1)S(1)} %all-gather.3) | copy-start | bytes 983044
  40.7 3.5 %copy-start.3 = (pred[4,9]{1,0:T(4,128)(4,1)S(1)}, pred[4,9]{1,0:T(4,128)(4,1)}, u32[]{:S(2)}) copy-start(pred[4,9]{1,0:T(4,128)(4,1)} %get-tuple-element.22) | copy-start | bytes 112
  40.7 4.0 %copy-start.2 = (bf16[4,10,4096]{2,1,0:T(8,128)(2,1)S(1)}, bf16[4,10,4096]{2,1,0:T(8,128)(2,1)}, u32[]{:S(2)}) copy-start(bf16[4,10,4096]{2,1,0:T(8,128)(2,1)} %copy-done.1) | copy-start | bytes 983044
  50.2 1.1 %copy-start = (bf16[1536,192]{0,1:T(8,128)(2,1)S(1)}, bf16[1536,192]{0,1:T(8,128)(2,1)}, u32[]{:S(2)}) copy-start(bf16[1536,192]{0,1:T(8,128)(2,1)} %reshape.301) | copy-start | bytes 1769476
  51.3 4.5 %copy-start.4 = (s32[1,13]{1,0:T(1,128)S(1)}, s32[1,13]{1,0:T(1,128)}, u32[]{:S(2)}) copy-start(s32[1,13]{1,0:T(1,128)} %param.7) | copy-start | bytes 160
  51.8 11.8 %collective-permute-start = (f32[384,192]{0,1:T(8,128)S(1)}, f32[384,192]{0,1:T(8,128)S(1)}, u32[]{:S(2)}, u32[]{:S(2)}) collective-permute-start(f32[384,192]{0,1:T(8,128)S(1)} %get-tuple-element.26), channel_id=1, source_target_pairs={{0,1},{1,2},{2,3},{3,0},{4,5},{5,6},{6,7},{7,4},{8,9},{9,10},{10,1... | collective-permute-start | bytes 884744 | tf_op jit(solution)/shard_map/ppermute | solution.py:71
  53.8 13.3 %collective-permute-start.1 = (f32[384,192]{0,1:T(8,128)S(1)}, f32[384,192]{0,1:T(8,128)S(1)}, u32[]{:S(2)}, u32[]{:S(2)}) collective-permute-start(f32[384,192]{0,1:T(8,128)S(1)} %get-tuple-element.26), channel_id=1, source_target_pairs={{0,3},{1,0},{2,1},{3,2},{4,7},{5,4},{6,5},{7,6},{8,11},{9,8},{10,9... | collective-permute-start | bytes 884744 | tf_op jit(solution)/shard_map/ppermute | solution.py:79
  63.6 10.5 %collective-permute-start.2 = (f32[384,192]{0,1:T(8,128)S(1)}, f32[384,192]{0,1:T(8,128)S(1)}, u32[]{:S(2)}, u32[]{:S(2)}) collective-permute-start(f32[384,192]{0,1:T(8,128)S(1)} %collective-permute-done), channel_id=1, source_target_pairs={{0,1},{1,2},{2,3},{3,0},{4,5},{5,6},{6,7},{7,4},{8,9},{9,10},{10,1... | collective-permute-start | bytes 884744 | tf_op jit(solution)/shard_map/ppermute | solution.py:71
